TPU v7x, 256 devices: a whole 4x4x8 slice. The times are simulated.
256 devices in a mesh: row: 8 (over y, core), col: 32 (over x, z).
Axes of the slice: x: 4, y: 4, z: 8, core: 2. Of those that a mesh axis runs over, the one named last changes fastest.
Arguments:
- hidden: bfloat16 [32768, 4608], P('col', 'row'), may hold values from -6 to 6
- w_query: bfloat16 [4608, 4096], P('col', 'row'), may hold values from -0.09375 to 0.09375
- w_key: bfloat16 [4608, 2048], P('col', 'row'), may hold values from -0.09375 to 0.09375
- w_value: bfloat16 [4608, 2048], P('col', 'row'), may hold values from -0.09375 to 0.09375
- adapter_down: bfloat16 [32, 4608, 32], P('col', 'row'), may hold values from -0.09375 to 0.09375
- adapter_up_query: bfloat16 [32, 16, 4096], P('col', None, 'row'), may hold values from -1.5 to 1.5
- adapter_up_value: bfloat16 [32, 16, 2048], P('col', None, 'row'), may hold values from -1.5 to 1.5
- lengths: int32 [32, 10], P('col'), may hold values from 1 to 192, 1024 in all within a row
- request_adapter: int32 [32, 10], P('col'), may hold values from 0 to 31
- adapter_slot: int32 [32], replicated, may hold values from 0 to 31, each once
- page_table: int32 [32, 18], P('col'), may hold values from 0 to 17, each once within a row
Outputs:
- query: bfloat16 [32768, 4096], P('col', 'row')
- key_cache: bfloat16 [576, 128, 2048], P('col', None, 'row')
- value_cache: bfloat16 [576, 128, 2048], P('col', None, 'row')
Inputs may be any that keep to these rules, and one draw needn't show every extreme that they name: Each row of lengths sums to 1024, and its longest request has exactly 192 tokens. `adapter_slot`: a permutation of the slots. `page_table`: each row is a permutation of the 18 local slots.
All inputs are finite; a program needn't handle non-finite values.
Results may differ from a plain program's by a relative error of at most 0.0039.
Values may be sent and summed in bfloat16 or wider, within the bound.
No kernel may reach another device: no remote copies, remote signals or barrier semaphores. Data moves between devices by JAX's collectives and lax.ppermute only.
A program may use at most 128 MiB of HBM per device.

v0:
```python
import math
import jax
import jax.numpy as jnp
from jax import lax
from jax.sharding import PartitionSpec as P

HEAD = 128
PAGE = 128
TOK_DEV = 1024


def rotate(values, cosine, sine_value):
    half_width = HEAD // 2
    shaped = values.reshape(values.shape[0], -1, HEAD)
    leading = shaped[:, :, :half_width]
    second = shaped[:, :, half_width:]
    rotated = jnp.concatenate(
        [leading * cosine - second * sine_value, second * cosine + leading * sine_value], axis=2
    )
    return rotated.reshape(values.shape)


def token_layout(lengths, chosen_request):
    token_index = jnp.arange(TOK_DEV, dtype=jnp.int32)
    starts = jnp.cumsum(lengths) - lengths
    inside = (token_index[:, None] >= starts[None, :]) & (
        token_index[:, None] < (starts + lengths)[None, :]
    )
    inside = inside.astype(jnp.int32)
    position = token_index - jnp.sum(inside * starts[None, :], axis=1)
    chosen = jnp.sum(inside * chosen_request[None, :], axis=1)
    return (starts, position, chosen)


def cache_rows(lengths, starts, page_row):
    pages = page_row.shape[0]
    pages_each = (lengths + PAGE - 1) // PAGE
    page_start = jnp.cumsum(pages_each) - pages_each
    page_ids = jnp.arange(pages, dtype=jnp.int32)
    owner = (page_row[:, None] == page_ids[None, :]).astype(jnp.int32)
    page_of_slot = jnp.sum(owner * page_ids[:, None], axis=0)
    member = (page_of_slot[:, None] >= page_start[None, :]) & (
        page_of_slot[:, None] < (page_start + pages_each)[None, :]
    )
    member = member.astype(jnp.int32)
    used = jnp.sum(member, axis=1) > 0
    first_page = jnp.sum(member * page_start[None, :], axis=1)
    first_token = jnp.sum(member * starts[None, :], axis=1)
    length = jnp.sum(member * lengths[None, :], axis=1)
    offset = (page_of_slot - first_page) * PAGE
    source = first_token + offset
    valid = jnp.where(used, jnp.minimum(length - offset, PAGE), 0)
    inner = jnp.arange(PAGE, dtype=jnp.int32)
    rows = (source[:, None] + inner[None, :]).reshape(-1)
    keep = (inner[None, :] < valid[:, None]).reshape(-1)
    rows = jnp.clip(rows, 0, TOK_DEV - 1)
    return (rows, keep)


def shards(
    hidden,
    w_query,
    w_key,
    w_value,
    adapter_down,
    adapter_up_query,
    adapter_up_value,
    lengths,
    request_adapter,
    adapter_slot,
    page_table,
):
    lengths = lengths[0]
    chosen_request = jnp.take(adapter_slot, request_adapter[0])
    starts, position, chosen = token_layout(lengths, chosen_request)
    adapter_count = adapter_slot.shape[0]
    rank_width = adapter_up_query.shape[1]
    query_width = w_query.shape[1]
    key_width = w_key.shape[1]
    weight_width = query_width + 2 * key_width
    feature_rows = w_query.shape[0]
    down_shape = adapter_down.shape[1:]
    row_size = lax.axis_size("row")
    with jax.named_scope("gathers"):
        full_rows = lax.all_gather(hidden, "row", axis=1, tiled=True)
        pieces = [
            jnp.concatenate([w_query, w_key, w_value], axis=1),
            adapter_down.reshape(-1, weight_width),
            adapter_up_query.reshape(-1, weight_width),
            adapter_up_value.reshape(-1, weight_width),
        ]
        bounds = [0]
        for piece in pieces:
            bounds.append(bounds[-1] + piece.shape[0])
        packed = lax.all_gather(jnp.concatenate(pieces, axis=0), "col", axis=0)
        weights = packed[:, : bounds[1]].reshape(-1, weight_width)
        down_local = packed[:, bounds[1] : bounds[2]].reshape((adapter_count,) + down_shape)
        up_query = packed[:, bounds[2] : bounds[3]].reshape(adapter_count, rank_width, -1)
        up_value = packed[:, bounds[3] : bounds[4]].reshape(adapter_count, rank_width, -1)
    with jax.named_scope("lowrank"):
        onehot = chosen[:, None] == jnp.arange(adapter_count, dtype=jnp.int32)[None, :]
        partial_all = jnp.einsum(
            "tf,sfr->tsr", hidden, down_local, preferred_element_type=jnp.float32
        )
        partial = jnp.sum(jnp.where(onehot[:, :, None], partial_all, 0.0), axis=1)
        distance = 1
        while distance < row_size:
            pairs = [(i, i ^ distance) for i in range(row_size)]
            partial = partial + lax.ppermute(partial, "row", pairs)
            distance *= 2
        lowrank = partial.astype(jnp.bfloat16)
        onehot_b = onehot.astype(jnp.bfloat16)
        spread_query = (onehot_b[:, :, None] * lowrank[:, None, :rank_width]).reshape(
            -1, adapter_count * rank_width
        )
        spread_value = (onehot_b[:, :, None] * lowrank[:, None, rank_width:]).reshape(
            -1, adapter_count * rank_width
        )
        delta_query = jnp.dot(
            spread_query,
            up_query.reshape(adapter_count * rank_width, -1),
            preferred_element_type=jnp.float32,
        )
        delta_value = jnp.dot(
            spread_value,
            up_value.reshape(adapter_count * rank_width, -1),
            preferred_element_type=jnp.float32,
        )
    with jax.named_scope("projection"):
        base = jnp.dot(full_rows, weights, preferred_element_type=jnp.float32)
        base_query = base[:, :query_width]
        base_key = base[:, query_width : query_width + key_width]
        base_value = base[:, query_width + key_width :]
    with jax.named_scope("rotary"):
        half_width = HEAD // 2
        frequency = jnp.exp(
            jnp.arange(half_width, dtype=jnp.float32) * (-2.0 * math.log(10000.0) / HEAD)
        )
        angles = position.astype(jnp.float32)[:, None] * frequency[None, :]
        cosine = jnp.cos(angles)[:, None, :]
        sine_value = jnp.sin(angles)[:, None, :]
        query = rotate(base_query + delta_query, cosine, sine_value).astype(jnp.bfloat16)
        key_rotated = rotate(base_key, cosine, sine_value).astype(jnp.bfloat16)
        value_rows = (base_value + delta_value).astype(jnp.bfloat16)
    with jax.named_scope("cache_write"):
        pages = page_table.shape[1]
        rows, keep = cache_rows(lengths, starts, page_table[0])
        key_cache = jnp.where(keep[:, None], jnp.take(key_rotated, rows, axis=0), 0).reshape(
            pages, PAGE, key_width
        )
        value_cache = jnp.where(keep[:, None], jnp.take(value_rows, rows, axis=0), 0).reshape(
            pages, PAGE, key_width
        )
    return (query, key_cache.astype(jnp.bfloat16), value_cache.astype(jnp.bfloat16))


def solution(mesh):
    return jax.shard_map(
        shards,
        mesh=mesh,
        in_specs=(
            P("col", "row"),
            P("col", "row"),
            P("col", "row"),
            P("col", "row"),
            P("col", "row", None),
            P("col", None, "row"),
            P("col", None, "row"),
            P("col", None),
            P("col", None),
            P(),
            P("col", None),
        ),
        out_specs=(P("col", "row"), P("col", None, "row"), P("col", None, "row")),
        check_vma=False,
    )
```

profile of v0, /device:TPU:1, one launch (start us, length us, event | category | flops | bytes accessed | tf_op | source)
XLA Modules:
  0.0 240.4 jit_solution(12034622873768710716)
XLA Ops:
  7.3 0.7 reshape.325
  8.0 0.7 reshape.324
  8.7 0.9 copy.31
  9.8 1.8 maximum_bitcast_fusion
  11.7 0.7 all-gather.5.cloned.1.call-update
  12.8 0.7 gather_fusion
  13.8 0.7 compare_and_fusion
  14.5 0.7 fusion.10
  15.2 1.0 multiply_cosine_fusion
  16.2 112.1 %all-gather.7.cloned.1.call-done = bf16[32,174,1024]{2,1,0:T(8,128)(2,1)} async-done(((bf16[1,174,1024]{2,1,0:T(8,128)(2,1)}), bf16[32,174,1024]{2,1,0:T(8,128)(2,1)}) %all-gather.7.cloned.1.call-update) | async-done | bytes 11403280 | tf_op jit(solution)/shard_map/gathers/all_gather | solution.py:95
  128.3 1.4 slice-done.3
  129.7 4.8 %reshape.328 = bf16[32,576,32]{2,1,0:T(8,128)(2,1)} reshape(bf16[32,18,1024]{2,1,0:T(8,128)(2,1)S(1)} %slice-done.3) | data formatting | bytes 2359296 | tf_op jit(solution)/shard_map/gathers/reshape | solution.py:97
  134.6 5.6 %fusion = f32[1024,32]{0,1:T(8,128)S(1)} fusion(bf16[32,576,32]{2,1,0:T(8,128)(2,1)} %reshape.328, pred[1024,32]{0,1:T(8,128)(4,1)S(1)} %get-tuple-element.23, bf16[1024,576]{0,1:T(8,128)(2,1)S(1)} %copy-done.2), kind=kOutput, calls=%fused_computation.4 | convolution fusion | flops 1210023936 | bytes 2523136 | tf_op jit(solution)/shard_map/lowrank/tf,sfr->tsr/dot_general | solution.py:102
  140.1 1.5 collective-permute-start
  141.6 0.6 fusion.4
  142.3 9.5 %slice.58 = bf16[32,144,1024]{2,1,0:T(8,128)(2,1)} slice(bf16[32,174,1024]{2,1,0:T(8,128)(2,1)} %all-gather.7.cloned.1.call-done), slice={[0:32], [0:144], [0:1024]} | slice | bytes 18874368 | tf_op jit(solution)/shard_map/gathers/slice | solution.py:96
  151.8 1.6 collective-permute-start.1
  153.4 33.7 %all-gather.5.cloned.1.call-done = bf16[1024,4608]{0,1:T(8,128)(2,1)} async-done(((bf16[1024,576]{0,1:T(8,128)(2,1)}), bf16[1024,4608]{0,1:T(8,128)(2,1)}) %all-gather.5.cloned.1.call-update) | async-done | bytes 9437200 | tf_op jit(solution)/shard_map/gathers/all_gather | solution.py:85
  187.1 14.7 %convolution_bitcast_fusion = f32[1024,1024]{0,1:T(8,128)S(1)} fusion(bf16[4608,1024]{1,0:T(8,128)(2,1)} %bitcast.63, bf16[1024,4608]{0,1:T(8,128)(2,1)} %all-gather.5.cloned.1.call-done), kind=kOutput, calls=%fused_computation.5 | convolution fusion | flops 9663676416 | bytes 23068672 | tf_op jit(solution)/shard_map/projection/dot_general | solution.py:130
  201.9 2.7 %collective-permute-start.2 = (f32[1024,32]{0,1:T(8,128)S(1)}, f32[1024,32]{0,1:T(8,128)S(1)}, u32[]{:S(2)}, u32[]{:S(2)}) collective-permute-start(f32[1024,32]{0,1:T(8,128)S(1)} %add.98), channel_id=1, source_target_pairs={{0,128},{32,160},{64,192},{96,224},{128,0},{160,32},{192,64},{224,... | collective-permute-start | bytes 393224 | tf_op jit(solution)/shard_map/lowrank/ppermute | solution.py:109
  205.2 1.4 slice.62
  206.6 1.0 reshape.329
  207.6 0.2 copy.40
  207.8 6.9 %gather_fusion.1 = bf16[2304,256]{1,0:T(8,128)(2,1)S(1)} fusion(bf16[1024,256]{1,0:T(8,128)(2,1)S(1)} %copy.40, s32[3072]{0:T(1024)S(1)} %pad_clamp_fusion), kind=kCustom, calls=%fused_computation.clone | custom fusion | bytes 2368512 | tf_op jit(solution)/shard_map/cache_write/jit(_take)/gather | solution.py:148
  214.7 1.0 broadcast_multiply_fusion
  215.7 2.5 %fusion.1 = bf16[1024,256]{0,1:T(8,128)(2,1)} fusion(bf16[1024,512]{0,1:T(8,128)(2,1)S(1)} %bitcast.68, bf16[512,256]{1,0:T(8,128)(2,1)S(1)} %reshape.333, f32[1024,1024]{0,1:T(8,128)} %copy-done.1), kind=kOutput, calls=%fused_computation.8 | convolution fusion | flops 268959744 | bytes 2883584 | tf_op jit(solution)/shard_map/lowrank/dot_general | solution.py:124
  218.2 1.2 copy.36
  219.5 2.5 %slice_add_fusion = f32[1024,512]{0,1:T(8,128)S(1)} fusion(f32[1024,1024]{0,1:T(8,128)} %copy-done.1, bf16[1024,512]{0,1:T(8,128)(2,1)S(1)} %bitcast.67, bf16[512,512]{1,0:T(8,128)(2,1)} %reshape.329), kind=kOutput, calls=%fused_computation.6 | convolution fusion | flops 537395200 | bytes 5767168 | tf_op jit(solution)/shard_map/lowrank/dot_general | solution.py:119
  222.0 0.3 subtract_convert_fusion
  222.5 1.3 copy.39
  223.8 6.9 %gather_fusion.2 = bf16[2304,256]{1,0:T(8,128)(2,1)S(1)} fusion(bf16[1024,256]{1,0:T(8,128)(2,1)S(1)} %copy.36, s32[3072]{0:T(1024)S(1)} %pad_clamp_fusion), kind=kCustom, calls=%fused_computation.1.clone | custom fusion | bytes 2368512 | tf_op jit(solution)/shard_map/cache_write/jit(_take)/gather | solution.py:151
  230.7 2.9 %select_select_fusion = (bf16[2304,256]{1,0:T(8,128)(2,1)}, bf16[2304,256]{1,0:T(8,128)(2,1)}) fusion(bf16[2304,256]{1,0:T(8,128)(2,1)S(1)} %gather_fusion.2, pred[2304]{0:T(1024)(128)(4,1)S(1)} %copy-done.3, pred[2304]{0:T(1024)(128)(4,1)S(1)} %copy-done.4, bf16[2304,256]{1,0:T(8,128)(2,1)S(1)} %gather_fusion.1), kind=kLoop, calls=%fused_computation.10 | loop fusion | flops 2359296 | bytes 4723200 | tf_op jit(solution)/shard_map/cache_write/jit(_where)/select_n | solution.py:151
  (55 shorter events, 1.9 us)
Async XLA Ops:
  7.2 5.6 %copy-start = (s32[32]{0:T(128)S(1)}, s32[32]{0:T(128)}, u32[]{:S(2)}) copy-start(s32[32]{0:T(128)} %param.22) | copy-start | bytes 388
  7.2 5.2 %copy-start.5 = (s32[1,10]{1,0:T(1,128)S(1)}, s32[1,10]{1,0:T(1,128)}, u32[]{:S(2)}) copy-start(s32[1,10]{1,0:T(1,128)} %param.20) | copy-start | bytes 124
  7.2 5.6 %copy-start.6 = (s32[1,10]{1,0:T(1,128)S(1)}, s32[1,10]{1,0:T(1,128)}, u32[]{:S(2)}) copy-start(s32[1,10]{1,0:T(1,128)} %param.21) | copy-start | bytes 124
  7.2 6.2 %copy-start.7 = (s32[1,18]{1,0:T(1,128)S(1)}, s32[1,18]{1,0:T(1,128)}, u32[]{:S(2)}) copy-start(s32[1,18]{1,0:T(1,128)} %param.23) | copy-start | bytes 220
  7.2 121.1 %all-gather.7.cloned.1.call-start = ((), (), s32[]{:S(2)}) async-start(), calls=%async_computation.1 | async-start | bytes 11894784 | tf_op jit(solution)/shard_map/gathers/all_gather | solution.py:95
  11.6 175.5 %all-gather.5.cloned.1.call-start = ((), (), s32[]{:S(2)}) async-start(), calls=%async_computation | async-start | bytes 10616832 | tf_op jit(solution)/shard_map/gathers/all_gather | solution.py:85
  128.3 1.4 slice-start.3
  129.7 4.9 %copy-start.2 = (bf16[1024,576]{0,1:T(8,128)(2,1)S(1)}, bf16[1024,576]{0,1:T(8,128)(2,1)}, u32[]{:S(2)}) copy-start(bf16[1024,576]{0,1:T(8,128)(2,1)} %param.13) | copy-start | bytes 3538948
  140.1 11.7 %collective-permute-start = (f32[1024,32]{0,1:T(8,128)S(1)}, f32[1024,32]{0,1:T(8,128)S(1)}, u32[]{:S(2)}, u32[]{:S(2)}) collective-permute-start(f32[1024,32]{0,1:T(8,128)S(1)} %fusion), channel_id=1, source_target_pairs={{0,32},{32,0},{64,96},{96,64},{128,160},{160,128},{192,224},{224,1... | collective-permute-start | bytes 393224 | tf_op jit(solution)/shard_map/lowrank/ppermute | solution.py:109
  151.8 50.1 %collective-permute-start.1 = (f32[1024,32]{0,1:T(8,128)S(1)}, f32[1024,32]{0,1:T(8,128)S(1)}, u32[]{:S(2)}, u32[]{:S(2)}) collective-permute-start(f32[1024,32]{0,1:T(8,128)S(1)} %add.97), channel_id=1, source_target_pairs={{0,64},{32,96},{64,0},{96,32},{128,192},{160,224},{192,128},{224,1... | collective-permute-start | bytes 393224 | tf_op jit(solution)/shard_map/lowrank/ppermute | solution.py:109
  187.1 17.7 %slice-start = ((s8[11534336]{0:T(1024)(128)(4,1)}), s8[4194304]{0:T(1024)(128)(4,1)S(1)}, s32[]{:S(2)}) async-start(s8[11534336]{0:T(1024)(128)(4,1)} %bitcast.61), calls=%async_computation.2 | async-start | bytes 8388608
  187.1 17.7 %slice-start.1 = ((s8[11534336]{0:T(1024)(128)(4,1)}), s8[4194304]{0:T(1024)(128)(4,1)S(1)}, s32[]{:S(2)}) async-start(s8[11534336]{0:T(1024)(128)(4,1)} %bitcast.61), calls=%async_computation.3 | async-start | bytes 8388608
  187.1 17.8 %slice-start.2 = ((s8[11534336]{0:T(1024)(128)(4,1)}), s8[3145728]{0:T(1024)(128)(4,1)S(1)}, s32[]{:S(2)}) async-start(s8[11534336]{0:T(1024)(128)(4,1)} %bitcast.61), calls=%async_computation.4 | async-start | bytes 6291456
  201.8 3.0 %copy-start.1 = (f32[1024,1024]{0,1:T(8,128)}, f32[1024,1024]{0,1:T(8,128)S(1)}, u32[]{:S(2)}) copy-start(f32[1024,1024]{0,1:T(8,128)S(1)} %convolution_bitcast_fusion) | copy-start | bytes 12582916
  201.9 12.8 %collective-permute-start.2 = (f32[1024,32]{0,1:T(8,128)S(1)}, f32[1024,32]{0,1:T(8,128)S(1)}, u32[]{:S(2)}, u32[]{:S(2)}) collective-permute-start(f32[1024,32]{0,1:T(8,128)S(1)} %add.98), channel_id=1, source_target_pairs={{0,128},{32,160},{64,192},{96,224},{128,0},{160,32},{192,64},{224,... | collective-permute-start | bytes 393224 | tf_op jit(solution)/shard_map/lowrank/ppermute | solution.py:109
  223.8 6.9 %copy-start.3 = (pred[2304]{0:T(1024)(128)(4,1)S(1)}, pred[2304]{0:T(1024)(128)(4,1)}, u32[]{:S(2)}) copy-start(pred[2304]{0:T(1024)(128)(4,1)} %compare_and_fusion) | copy-start | bytes 6916
  223.8 6.9 %copy-start.4 = (pred[2304]{0:T(1024)(128)(4,1)S(1)}, pred[2304]{0:T(1024)(128)(4,1)}, u32[]{:S(2)}) copy-start(pred[2304]{0:T(1024)(128)(4,1)} %fusion.4) | copy-start | bytes 6916
Sparse Core Ops, SparseCore 0:
  11.7 116.5 all-gather.6
  130.1 56.9 all-gather.4
where the time goes:
time: 241 us; the launch traced here: 240 us
  waiting for transfers between devices  147 us (61%)
  local copies, waits for them, and re-layouts  38.3 us (16%)
  matrix products  25.3 us (10%)
  between operations  14.4 us (6%)
  other arithmetic  10 us (4%)
  starting transfers between devices  5.83 us (2%)
    all_gather x1, waiting for transfers between devices, shards(): packed = lax.all_gather(jnp.concatenate(pieces, axis=0), 'col', axis=0)  112 us
    all_gather x1, waiting for transfers between devices, shards(): full_rows = lax.all_gather(hidden, 'row', axis=1, tiled=True)  33.7 us
    dot_general x1, matrix products, shards(): base = jnp.dot(full_rows, weights, preferred_element_type=jnp.float32)  14.7 us
    slice x1, local copies, waits for them, and re-layouts, shards(): weights = packed[:, :bounds[1]].reshape(-1, weight_width)  9.52 us
    gather x1, local copies, waits for them, and re-layouts, shards(): jnp.take(key_rotated, rows, axis=0)  6.86 us
    gather x1, local copies, waits for them, and re-layouts, shards(): jnp.take(value_rows, rows, axis=0)  6.86 us
    ppermute x3, starting transfers between devices, shards(): partial = partial + lax.ppermute(partial, 'row', pairs)  5.75 us
    dot_general x1, matrix products, shards(): jnp.einsum('tf,sfr->tsr', hidden, down_local, preferred_element_type=jnp....  5.55 us
  transfers between devices with their start and end apart: 5, of which 2 were waited for; matrix products, arithmetic and copies ran while one was open for 20% of the time, Pallas kernels for 0%

commit v1 on v0

--- a/solution.py
+++ b/solution.py
@@ -82,7 +82,9 @@
     down_shape = adapter_down.shape[1:]
     row_size = lax.axis_size("row")
     with jax.named_scope("gathers"):
-        full_rows = lax.all_gather(hidden, "row", axis=1, tiled=True)
+        full_rows = jnp.concatenate(
+            lax.all_to_all(jnp.stack([hidden] * lax.axis_size("row")), "row", 0, 0), axis=1
+        )
         pieces = [
             jnp.concatenate([w_query, w_key, w_value], axis=1),
             adapter_down.reshape(-1, weight_width),

time: 241 us -> 206 us (0.85)
  waiting for transfers between devices: 147 us -> 99.7 us
  starting transfers between devices: 5.83 us -> 13.8 us
  local copies, waits for them, and re-layouts: 38.3 us -> 42.7 us
    all_gather x1 -> x0, waiting for transfers between devices: 33.7 us -> none  [shards(): full_rows = lax.all_gather(hidden, 'row', axis=1, tiled=True)]
    all_gather x1, waiting for transfers between devices: 112 us -> 99.7 us  [shards(): packed = lax.all_gather(jnp.concatenate(pieces, axis=0), 'col', axis=0)]
    all_to_all x0 -> x1, starting transfers between devices: none -> 8.27 us  [shards(): lax.all_to_all(jnp.stack([hidden] * lax.axis_size('row')), 'row', 0, 0)]
    another operation x0 -> x1, local copies, waits for them, and re-layouts: none -> 4.86 us  [shards(): jnp.stack([hidden] * lax.axis_size('row'))]
  transfers between devices with their start and end apart: 5 -> 5, of which waited for: 2 -> 1; matrix products, arithmetic and copies ran while one was open for 20% -> 26% of each run, Pallas kernels for 0% -> 0%
where the time goes in v1:
time: 206 us
  waiting for transfers between devices  99.7 us (48%)
  local copies, waits for them, and re-layouts  42.7 us (21%)
  matrix products  25.3 us (12%)
  between operations  14.3 us (7%)
  starting transfers between devices  13.8 us (7%)
  other arithmetic  10 us (5%)
    all_gather x1, waiting for transfers between devices, shards(): packed = lax.all_gather(jnp.concatenate(pieces, axis=0), 'col', axis=0)  99.7 us
    dot_general x1, matrix products, shards(): base = jnp.dot(full_rows, weights, preferred_element_type=jnp.float32)  14.7 us
    slice x1, local copies, waits for them, and re-layouts, shards(): weights = packed[:, :bounds[1]].reshape(-1, weight_width)  9.06 us
    all_to_all x1, starting transfers between devices, shards(): lax.all_to_all(jnp.stack([hidden] * lax.axis_size('row')), 'row', 0, 0)  8.27 us
    gather x1, local copies, waits for them, and re-layouts, shards(): jnp.take(key_rotated, rows, axis=0)  6.86 us
    gather x1, local copies, waits for them, and re-layouts, shards(): jnp.take(value_rows, rows, axis=0)  6.86 us
    dot_general x1, matrix products, shards(): jnp.einsum('tf,sfr->tsr', hidden, down_local, preferred_element_type=jnp....  5.55 us
    ppermute x3, starting transfers between devices, shards(): partial = partial + lax.ppermute(partial, 'row', pairs)  5.48 us
  transfers between devices with their start and end apart: 5, of which 1 were waited for; matrix products, arithmetic and copies ran while one was open for 26% of the time, Pallas kernels for 0%

profile of v1, /device:TPU:1, one launch (start us, length us, event | category | flops | bytes accessed | tf_op | source)
XLA Modules:
  0.0 205.9 jit_solution(864731133769735872)
XLA Ops:
  7.2 0.8 reshape.333
  8.0 0.7 reshape.332
  8.8 0.9 copy.32
  9.9 1.8 maximum_bitcast_fusion
  11.7 4.9 %stack.2 = bf16[8,1024,576]{1,2,0:T(8,128)(2,1)} broadcast(bf16[1024,576]{0,1:T(8,128)(2,1)S(1)} %copy-done.3), dimensions={1,2} | broadcast | bytes 10616832 | tf_op jit(solution)/shard_map/gathers/stack | solution.py:86
  16.6 8.3 %all-to-all-start = ((bf16[8,1024,576]{1,2,0:T(8,128)(2,1)}), bf16[8,1024,576]{1,2,0:T(8,128)(2,1)}, u32[]{:S(2)}, u32[]{:S(2)}) async-start(bf16[8,1024,576]{1,2,0:T(8,128)(2,1)} %stack.2), calls=%async_computation | async-start | bytes 18874368 | tf_op jit(solution)/shard_map/gathers/all_to_all | solution.py:86
  25.2 0.7 gather_fusion
  26.2 0.7 compare_and_fusion
  27.0 0.7 fusion.10
  27.6 1.0 multiply_cosine_fusion
  28.6 99.7 %all-gather.4.cloned.1.call-done = bf16[32,174,1024]{2,1,0:T(8,128)(2,1)} async-done(((bf16[1,174,1024]{2,1,0:T(8,128)(2,1)}), bf16[32,174,1024]{2,1,0:T(8,128)(2,1)}) %all-gather.4.cloned.1.call-update) | async-done | bytes 11403280 | tf_op jit(solution)/shard_map/gathers/all_gather | solution.py:97
  128.3 1.4 slice-done.3
  129.7 4.7 %reshape.338 = bf16[32,576,32]{2,1,0:T(8,128)(2,1)} reshape(bf16[32,18,1024]{2,1,0:T(8,128)(2,1)S(1)} %slice-done.3) | data formatting | bytes 2359296 | tf_op jit(solution)/shard_map/gathers/reshape | solution.py:99
  134.5 5.6 %fusion = f32[1024,32]{0,1:T(8,128)S(1)} fusion(bf16[32,576,32]{2,1,0:T(8,128)(2,1)} %reshape.338, pred[1024,32]{0,1:T(8,128)(4,1)S(1)} %get-tuple-element.23, bf16[1024,576]{0,1:T(8,128)(2,1)S(1)} %copy-done.3), kind=kOutput, calls=%fused_computation.4 | convolution fusion | flops 1210023936 | bytes 2523136 | tf_op jit(solution)/shard_map/lowrank/tf,sfr->tsr/dot_general | solution.py:104
  140.0 1.5 collective-permute-start
  141.5 0.6 fusion.4
  142.2 9.1 %slice.58 = bf16[32,144,1024]{2,1,0:T(8,128)(2,1)} slice(bf16[32,174,1024]{2,1,0:T(8,128)(2,1)} %all-gather.4.cloned.1.call-done), slice={[0:32], [0:144], [0:1024]} | slice | bytes 18874368 | tf_op jit(solution)/shard_map/gathers/slice | solution.py:98
  151.3 1.3 collective-permute-start.1
  152.6 14.7 %convolution_bitcast_fusion = f32[1024,1024]{0,1:T(8,128)S(1)} fusion(bf16[4608,1024]{1,0:T(8,128)(2,1)} %bitcast.66, bf16[1024,4608]{0,1:T(8,128)(2,1)} %bitcast.3), kind=kOutput, calls=%fused_computation.5 | convolution fusion | flops 9663676416 | bytes 23068672 | tf_op jit(solution)/shard_map/projection/dot_general | solution.py:132
  167.4 2.7 %collective-permute-start.2 = (f32[1024,32]{0,1:T(8,128)S(1)}, f32[1024,32]{0,1:T(8,128)S(1)}, u32[]{:S(2)}, u32[]{:S(2)}) collective-permute-start(f32[1024,32]{0,1:T(8,128)S(1)} %add.98), channel_id=1, source_target_pairs={{0,128},{32,160},{64,192},{96,224},{128,0},{160,32},{192,64},{224,... | collective-permute-start | bytes 393224 | tf_op jit(solution)/shard_map/lowrank/ppermute | solution.py:111
  170.7 1.4 slice.62
  172.1 1.0 reshape.339
  173.1 0.2 copy.41
  173.3 6.9 %gather_fusion.1 = bf16[2304,256]{1,0:T(8,128)(2,1)S(1)} fusion(bf16[1024,256]{1,0:T(8,128)(2,1)S(1)} %copy.41, s32[3072]{0:T(1024)S(1)} %pad_clamp_fusion), kind=kCustom, calls=%fused_computation.clone | custom fusion | bytes 2368512 | tf_op jit(solution)/shard_map/cache_write/jit(_take)/gather | solution.py:150
  180.2 1.0 broadcast_multiply_fusion
  181.2 2.5 %fusion.1 = bf16[1024,256]{0,1:T(8,128)(2,1)} fusion(bf16[1024,512]{0,1:T(8,128)(2,1)S(1)} %bitcast.71, bf16[512,256]{1,0:T(8,128)(2,1)S(1)} %reshape.343, f32[1024,1024]{0,1:T(8,128)} %copy-done.2), kind=kOutput, calls=%fused_computation.8 | convolution fusion | flops 268959744 | bytes 2883584 | tf_op jit(solution)/shard_map/lowrank/dot_general | solution.py:126
  183.7 1.2 copy.37
  185.0 2.5 %slice_add_fusion = f32[1024,512]{0,1:T(8,128)S(1)} fusion(f32[1024,1024]{0,1:T(8,128)} %copy-done.2, bf16[1024,512]{0,1:T(8,128)(2,1)S(1)} %bitcast.70, bf16[512,512]{1,0:T(8,128)(2,1)} %reshape.339), kind=kOutput, calls=%fused_computation.6 | convolution fusion | flops 537395200 | bytes 5767168 | tf_op jit(solution)/shard_map/lowrank/dot_general | solution.py:121
  187.5 0.3 subtract_convert_fusion
  187.9 1.3 copy.40
  189.3 6.9 %gather_fusion.2 = bf16[2304,256]{1,0:T(8,128)(2,1)S(1)} fusion(bf16[1024,256]{1,0:T(8,128)(2,1)S(1)} %copy.37, s32[3072]{0:T(1024)S(1)} %pad_clamp_fusion), kind=kCustom, calls=%fused_computation.1.clone | custom fusion | bytes 2368512 | tf_op jit(solution)/shard_map/cache_write/jit(_take)/gather | solution.py:153
  196.2 2.9 %select_select_fusion = (bf16[2304,256]{1,0:T(8,128)(2,1)}, bf16[2304,256]{1,0:T(8,128)(2,1)}) fusion(bf16[2304,256]{1,0:T(8,128)(2,1)S(1)} %gather_fusion.2, pred[2304]{0:T(1024)(128)(4,1)S(1)} %copy-done.4, pred[2304]{0:T(1024)(128)(4,1)S(1)} %copy-done.5, bf16[2304,256]{1,0:T(8,128)(2,1)S(1)} %gather_fusion.1), kind=kLoop, calls=%fused_computation.10 | loop fusion | flops 2359296 | bytes 4723200 | tf_op jit(solution)/shard_map/cache_write/jit(_where)/select_n | solution.py:153
  (57 shorter events, 1.8 us)
Async XLA Ops:
  7.2 18.1 %copy-start = (s32[32]{0:T(128)S(1)}, s32[32]{0:T(128)}, u32[]{:S(2)}) copy-start(s32[32]{0:T(128)} %param.22) | copy-start | bytes 388
  7.2 4.5 %copy-start.3 = (bf16[1024,576]{0,1:T(8,128)(2,1)S(1)}, bf16[1024,576]{0,1:T(8,128)(2,1)}, u32[]{:S(2)}) copy-start(bf16[1024,576]{0,1:T(8,128)(2,1)} %param.13) | copy-start | bytes 3538948
  7.2 121.1 %all-gather.4.cloned.1.call-start = ((), (), s32[]{:S(2)}) async-start(), calls=%async_computation.1 | async-start | bytes 11894784 | tf_op jit(solution)/shard_map/gathers/all_gather | solution.py:97
  16.5 8.3 %copy-start.6 = (s32[1,10]{1,0:T(1,128)S(1)}, s32[1,10]{1,0:T(1,128)}, u32[]{:S(2)}) copy-start(s32[1,10]{1,0:T(1,128)} %param.20) | copy-start | bytes 124
  16.5 8.7 %copy-start.7 = (s32[1,10]{1,0:T(1,128)S(1)}, s32[1,10]{1,0:T(1,128)}, u32[]{:S(2)}) copy-start(s32[1,10]{1,0:T(1,128)} %param.21) | copy-start | bytes 124
  16.6 9.4 %copy-start.8 = (s32[1,18]{1,0:T(1,128)S(1)}, s32[1,18]{1,0:T(1,128)}, u32[]{:S(2)}) copy-start(s32[1,18]{1,0:T(1,128)} %param.23) | copy-start | bytes 220
  16.6 136.0 %all-to-all-start = ((bf16[8,1024,576]{1,2,0:T(8,128)(2,1)}), bf16[8,1024,576]{1,2,0:T(8,128)(2,1)}, u32[]{:S(2)}, u32[]{:S(2)}) async-start(bf16[8,1024,576]{1,2,0:T(8,128)(2,1)} %stack.2), calls=%async_computation | async-start | bytes 18874368 | tf_op jit(solution)/shard_map/gathers/all_to_all | solution.py:86
  128.3 1.4 slice-start.3
  140.0 11.2 %collective-permute-start = (f32[1024,32]{0,1:T(8,128)S(1)}, f32[1024,32]{0,1:T(8,128)S(1)}, u32[]{:S(2)}, u32[]{:S(2)}) collective-permute-start(f32[1024,32]{0,1:T(8,128)S(1)} %fusion), channel_id=1, source_target_pairs={{0,32},{32,0},{64,96},{96,64},{128,160},{160,128},{192,224},{224,1... | collective-permute-start | bytes 393224 | tf_op jit(solution)/shard_map/lowrank/ppermute | solution.py:111
  151.3 16.1 %collective-permute-start.1 = (f32[1024,32]{0,1:T(8,128)S(1)}, f32[1024,32]{0,1:T(8,128)S(1)}, u32[]{:S(2)}, u32[]{:S(2)}) collective-permute-start(f32[1024,32]{0,1:T(8,128)S(1)} %add.97), channel_id=1, source_target_pairs={{0,64},{32,96},{64,0},{96,32},{128,192},{160,224},{192,128},{224,1... | collective-permute-start | bytes 393224 | tf_op jit(solution)/shard_map/lowrank/ppermute | solution.py:111
  152.6 17.7 %slice-start = ((s8[11534336]{0:T(1024)(128)(4,1)}), s8[4194304]{0:T(1024)(128)(4,1)S(1)}, s32[]{:S(2)}) async-start(s8[11534336]{0:T(1024)(128)(4,1)} %bitcast.64), calls=%async_computation.2 | async-start | bytes 8388608
  152.6 17.8 %slice-start.1 = ((s8[11534336]{0:T(1024)(128)(4,1)}), s8[4194304]{0:T(1024)(128)(4,1)S(1)}, s32[]{:S(2)}) async-start(s8[11534336]{0:T(1024)(128)(4,1)} %bitcast.64), calls=%async_computation.3 | async-start | bytes 8388608
  152.6 17.8 %slice-start.2 = ((s8[11534336]{0:T(1024)(128)(4,1)}), s8[3145728]{0:T(1024)(128)(4,1)S(1)}, s32[]{:S(2)}) async-start(s8[11534336]{0:T(1024)(128)(4,1)} %bitcast.64), calls=%async_computation.4 | async-start | bytes 6291456
  167.3 3.0 %copy-start.2 = (f32[1024,1024]{0,1:T(8,128)}, f32[1024,1024]{0,1:T(8,128)S(1)}, u32[]{:S(2)}) copy-start(f32[1024,1024]{0,1:T(8,128)S(1)} %convolution_bitcast_fusion) | copy-start | bytes 12582916
  167.4 12.8 %collective-permute-start.2 = (f32[1024,32]{0,1:T(8,128)S(1)}, f32[1024,32]{0,1:T(8,128)S(1)}, u32[]{:S(2)}, u32[]{:S(2)}) collective-permute-start(f32[1024,32]{0,1:T(8,128)S(1)} %add.98), channel_id=1, source_target_pairs={{0,128},{32,160},{64,192},{96,224},{128,0},{160,32},{192,64},{224,... | collective-permute-start | bytes 393224 | tf_op jit(solution)/shard_map/lowrank/ppermute | solution.py:111
  189.3 6.9 %copy-start.4 = (pred[2304]{0:T(1024)(128)(4,1)S(1)}, pred[2304]{0:T(1024)(128)(4,1)}, u32[]{:S(2)}) copy-start(pred[2304]{0:T(1024)(128)(4,1)} %compare_and_fusion) | copy-start | bytes 6916
  189.3 6.9 %copy-start.5 = (pred[2304]{0:T(1024)(128)(4,1)S(1)}, pred[2304]{0:T(1024)(128)(4,1)}, u32[]{:S(2)}) copy-start(pred[2304]{0:T(1024)(128)(4,1)} %fusion.4) | copy-start | bytes 6916
  189.3 9.8 %copy-start.1 = (s32[32]{0:T(128)S(1)}, s32[32]{0:T(128)}, u32[]{:S(2)}) copy-start(s32[32]{0:T(128)} %param.22) | copy-start | bytes 388
Sparse Core Ops, SparseCore 0:
  11.8 116.4 all-gather.3
